TPU v7x, 512 devices: a whole 4x8x8 slice. The times are simulated.
512 devices in a mesh: tm: 64 (over y, x, core), head: 8 (over z).
Axes of the slice: x: 4, y: 8, z: 8, core: 2. Of those that a mesh axis runs over, the one named last changes fastest.
Arguments:
- queries: bfloat16 [24576, 5120], P('tm', 'head')
- keys: bfloat16 [24576, 5120], P('tm', 'head')
- values: bfloat16 [24576, 5120], P('tm', 'head')
- text_keys: bfloat16 [512, 5120], P('tm', 'head'), may hold values from -6 to 6
- text_values: bfloat16 [512, 5120], P('tm', 'head')
- out_weight: bfloat16 [5120, 5120], P('head', 'tm'), may hold values from -0.25 to 0.25
- windows: int32 [64], replicated, may hold values from 0 to 4, as said below
- lengths: int32 [64], replicated, may hold values from 96 to 384, as said below
Outputs:
- mixed: bfloat16 [24576, 5120], P('tm', 'head')
Inputs may be any that keep to these rules, and one draw needn't show every extreme that they name: windows reach 4 for some frame in every draw. `lengths`: some frame is full in every draw.
All inputs are finite; a program needn't handle non-finite values.
Results may differ from a plain program's by a relative error of at most 0.014.
Values may be sent and summed in bfloat16 or wider, within the bound.
No kernel may reach another device: no remote copies, remote signals or barrier semaphores. Data moves between devices by JAX's collectives and lax.ppermute only.
A program may use at most 64 MiB of HBM per device.

v0:
```python
import math
import jax
import jax.numpy as jnp
from jax import lax
from jax.sharding import PartitionSpec as P

HD = 128
WIN = 4


def from_behind(value, axis, steps):
    count = lax.axis_size(axis)
    initial, last = (max(0, -steps), min(count, count - steps))
    return lax.ppermute(value, axis, [(source, source + steps) for source in range(initial, last)])


def on_device(queries, keys, values, text_keys, text_values, out_weight, windows, lengths):
    rows = queries.shape[0]
    width = queries.shape[1]
    local_heads = width // HD
    scale = 1.0 / math.sqrt(HD)
    position = lax.axis_index("tm")
    text_k, text_v = (
        lax.all_gather(text_keys, "tm", axis=0, tiled=True),
        lax.all_gather(text_values, "tm", axis=0, tiled=True),
    )
    key_list = [keys]
    value_list = [values]
    for step in range(1, WIN + 1):
        moved_k, moved_v = from_behind((keys, values), "tm", step)
        key_list.append(moved_k)
        value_list.append(moved_v)
    token_ids = jnp.arange(rows, dtype=jnp.int32)
    own_window = windows[position]
    mask_list = []
    for step in range(WIN + 1):
        source = position - step
        usable = (step <= own_window) & (source >= 0)
        source_len = lengths[jnp.maximum(source, 0)]
        mask_list.append(usable & (token_ids < source_len))
    mask_list.append(jnp.ones((text_k.shape[0],), bool))
    key_mask = jnp.concatenate(mask_list)
    all_keys = jnp.concatenate(key_list + [text_k], axis=0)
    all_values = jnp.concatenate(value_list + [text_v], axis=0)
    head_outputs = []
    for head_index in range(local_heads):
        lower = head_index * HD
        query_h = queries[:, lower : lower + HD]
        key_h = all_keys[:, lower : lower + HD]
        value_h = all_values[:, lower : lower + HD]
        scores = (
            lax.dot_general(
                query_h, key_h, (((1,), (1,)), ((), ())), preferred_element_type=jnp.float32
            )
            * scale
        )
        scores = jnp.where(key_mask[None, :], scores, -jnp.inf)
        top = jnp.max(scores, axis=-1, keepdims=True)
        weights = jnp.exp(scores - top)
        total = jnp.sum(weights, axis=-1, keepdims=True)
        attended = (
            jnp.dot(weights.astype(jnp.bfloat16), value_h, preferred_element_type=jnp.float32)
            / total
        )
        head_outputs.append(attended.astype(jnp.bfloat16))
    attended_all = jnp.concatenate(head_outputs, axis=1)
    partial_out = jnp.dot(
        attended_all,
        lax.all_gather(out_weight, "tm", axis=1, tiled=True),
        preferred_element_type=jnp.float32,
    )
    return lax.psum_scatter(
        partial_out.astype(jnp.bfloat16), "head", scatter_dimension=1, tiled=True
    )


def solution(mesh):
    return jax.shard_map(
        on_device,
        mesh=mesh,
        in_specs=(
            P("tm", "head"),
            P("tm", "head"),
            P("tm", "head"),
            P("tm", "head"),
            P("tm", "head"),
            P("head", "tm"),
            P(),
            P(),
        ),
        out_specs=P("tm", "head"),
        check_vma=False,
    )
```

profile of v0, /device:TPU:1, one launch (start us, length us, event | category | flops | bytes accessed | tf_op | source)
XLA Modules:
  0.0 300.5 jit_solution(977108429921644657)
XLA Ops:
  7.3 4.5 %collective-permute-start = (bf16[384,640]{1,0:T(8,128)(2,1)}, bf16[384,640]{1,0:T(8,128)(2,1)S(1)}, u32[]{:S(2)}, u32[]{:S(2)}) collective-permute-start(bf16[384,640]{1,0:T(8,128)(2,1)} %param.9), channel_id=1, source_target_pairs={{0,8},{8,16},{16,24},{24,32},{32,40},{40,48},{48,56},{56,64},{64,7... | collective-permute-start | bytes 1474568 | tf_op jit(solution)/shard_map/ppermute | solution.py:14
  11.8 3.1 %collective-permute-start.1 = (bf16[384,640]{1,0:T(8,128)(2,1)}, bf16[384,640]{1,0:T(8,128)(2,1)S(1)}, u32[]{:S(2)}, u32[]{:S(2)}) collective-permute-start(bf16[384,640]{1,0:T(8,128)(2,1)} %param.9), channel_id=1, source_target_pairs={{0,16},{8,24},{16,32},{24,40},{32,48},{40,56},{48,64},{56,72},{64,... | collective-permute-start | bytes 1474568 | tf_op jit(solution)/shard_map/ppermute | solution.py:14
  15.0 3.4 %collective-permute-start.2 = (bf16[384,640]{1,0:T(8,128)(2,1)}, bf16[384,640]{1,0:T(8,128)(2,1)S(1)}, u32[]{:S(2)}, u32[]{:S(2)}) collective-permute-start(bf16[384,640]{1,0:T(8,128)(2,1)} %param.9), channel_id=1, source_target_pairs={{0,24},{8,32},{16,40},{24,48},{32,56},{40,64},{48,72},{56,80},{64,... | collective-permute-start | bytes 1474568 | tf_op jit(solution)/shard_map/ppermute | solution.py:14
  18.4 3.4 %collective-permute-start.3 = (bf16[384,640]{1,0:T(8,128)(2,1)}, bf16[384,640]{1,0:T(8,128)(2,1)S(1)}, u32[]{:S(2)}, u32[]{:S(2)}) collective-permute-start(bf16[384,640]{1,0:T(8,128)(2,1)} %param.9), channel_id=1, source_target_pairs={{0,32},{8,40},{16,48},{24,56},{32,64},{40,72},{48,80},{56,88},{64,... | collective-permute-start | bytes 1474568 | tf_op jit(solution)/shard_map/ppermute | solution.py:14
  21.9 3.7 %collective-permute-start.4 = (bf16[384,640]{1,0:T(8,128)(2,1)}, bf16[384,640]{1,0:T(8,128)(2,1)S(1)}, u32[]{:S(2)}, u32[]{:S(2)}) collective-permute-start(bf16[384,640]{1,0:T(8,128)(2,1)} %param.10), channel_id=1, source_target_pairs={{0,8},{8,16},{16,24},{24,32},{32,40},{40,48},{48,56},{56,64},{64,7... | collective-permute-start | bytes 1474568 | tf_op jit(solution)/shard_map/ppermute | solution.py:14
  25.6 1.2 dynamic_slice.18
  30.1 1.5 fusion.95
  36.3 74.3 %all_gather.9 = bf16[512,640]{1,0:T(8,128)(2,1)S(1)} all-gather(bf16[8,640]{1,0:T(8,128)(2,1)} %param.11), channel_id=1, replica_groups=mesh['tm'=64,'head'=8] {'tm'}, dimensions={0}, use_global_device_ids=true | all-gather | bytes 665600 | tf_op jit(solution)/shard_map/all_gather | solution.py:24
  110.6 48.6 %all_gather.10 = bf16[512,640]{1,0:T(8,128)(2,1)S(1)} all-gather(bf16[8,640]{1,0:T(8,128)(2,1)} %param.12), channel_id=1, replica_groups=mesh['tm'=64,'head'=8] {'tm'}, dimensions={0}, use_global_device_ids=true | all-gather | bytes 665600 | tf_op jit(solution)/shard_map/all_gather | solution.py:25
  159.3 1.1 constant_dynamic-update-slice_fusion.5
  160.3 1.1 constant_dynamic-update-slice_fusion.11
  161.4 2.3 collective-permute-start.5
  163.8 4.6 %collective-permute-start.6 = (bf16[384,640]{1,0:T(8,128)(2,1)S(1)}, bf16[384,640]{1,0:T(8,128)(2,1)S(1)}, u32[]{:S(2)}, u32[]{:S(2)}) collective-permute-start(bf16[384,640]{1,0:T(8,128)(2,1)S(1)} %copy-done), channel_id=1, source_target_pairs={{0,24},{8,32},{16,40},{24,48},{32,56},{40,64},{48,72},{56,80},{64,... | collective-permute-start | bytes 1474568 | tf_op jit(solution)/shard_map/ppermute | solution.py:14
  168.6 2.3 collective-permute-start.7
  171.1 3.4 %collective-permute-done.5 = bf16[384,640]{1,0:T(8,128)(2,1)S(1)} collective-permute-done((bf16[384,640]{1,0:T(8,128)(2,1)}, bf16[384,640]{1,0:T(8,128)(2,1)S(1)}, u32[]{:S(2)}, u32[]{:S(2)}) %collective-permute-start.5) | collective-permute-done | bytes 491552 | tf_op jit(solution)/shard_map/ppermute | solution.py:14
  174.5 10.4 %collective-permute-done.6 = bf16[384,640]{1,0:T(8,128)(2,1)S(1)} collective-permute-done((bf16[384,640]{1,0:T(8,128)(2,1)S(1)}, bf16[384,640]{1,0:T(8,128)(2,1)S(1)}, u32[]{:S(2)}, u32[]{:S(2)}) %collective-permute-start.6) | collective-permute-done | bytes 491552 | tf_op jit(solution)/shard_map/ppermute | solution.py:14
  185.0 10.5 %collective-permute-done.7 = bf16[384,640]{1,0:T(8,128)(2,1)S(1)} collective-permute-done((bf16[384,640]{1,0:T(8,128)(2,1)S(1)}, bf16[384,640]{1,0:T(8,128)(2,1)S(1)}, u32[]{:S(2)}, u32[]{:S(2)}) %collective-permute-start.7) | collective-permute-done | bytes 491552 | tf_op jit(solution)/shard_map/ppermute | solution.py:14
  195.7 0.9 fusion.96
  198.8 0.9 fusion.98
  201.8 0.9 fusion.100
  207.1 8.9 %convolution_convert_fusion = bf16[384,5120]{1,0:T(8,128)(2,1)} fusion(bf16[384,640]{1,0:T(8,128)(2,1)S(1)} %fusion.48, bf16[640,5120]{0,1:T(8,128)(2,1)} %all-gather.2.cloned.1.call-done), kind=kOutput, calls=%fused_computation | convolution fusion | flops 2518548480 | bytes 10977280 | tf_op jit(solution)/shard_map/dot_general | solution.py:67
  216.1 6.3 %copy.9 = bf16[384,5120]{0,1:T(8,128)(2,1)} copy(bf16[384,5120]{1,0:T(8,128)(2,1)} %convolution_convert_fusion) | data formatting | bytes 7864320
  222.4 69.3 %reduce-scatter.4.cloned.1.call-done = bf16[640,384]{1,0:T(8,128)(2,1)} async-done(((bf16[5120,384]{1,0:T(8,128)(2,1)}), bf16[640,384]{1,0:T(8,128)(2,1)}) %reduce-scatter.4.cloned.1.call-update) | async-done | bytes 491536
  291.6 2.0 copy.10
  (49 shorter events, 14.8 us)
Async XLA Ops:
  6.5 157.3 %copy-start = (bf16[384,640]{1,0:T(8,128)(2,1)S(1)}, bf16[384,640]{1,0:T(8,128)(2,1)}, u32[]{:S(2)}) copy-start(bf16[384,640]{1,0:T(8,128)(2,1)} %param.10) | copy-start | bytes 1474564
  6.5 200.6 %all-gather.2.cloned.1.call-start = ((), (), s32[]{:S(2)}) async-start(), calls=%async_computation.1 | async-start | bytes 6656000 | tf_op jit(solution)/shard_map/all_gather | solution.py:69
  7.3 284.4 %reduce-scatter.4.cloned.1.call-start = ((), (), s32[]{:S(2)}) async-start(), calls=%async_computation.2 | async-start | bytes 4423680
  7.3 154.1 %collective-permute-start = (bf16[384,640]{1,0:T(8,128)(2,1)}, bf16[384,640]{1,0:T(8,128)(2,1)S(1)}, u32[]{:S(2)}, u32[]{:S(2)}) collective-permute-start(bf16[384,640]{1,0:T(8,128)(2,1)} %param.9), channel_id=1, source_target_pairs={{0,8},{8,16},{16,24},{24,32},{32,40},{40,48},{48,56},{56,64},{64,7... | collective-permute-start | bytes 1474568 | tf_op jit(solution)/shard_map/ppermute | solution.py:14
  11.8 152.0 %collective-permute-start.1 = (bf16[384,640]{1,0:T(8,128)(2,1)}, bf16[384,640]{1,0:T(8,128)(2,1)S(1)}, u32[]{:S(2)}, u32[]{:S(2)}) collective-permute-start(bf16[384,640]{1,0:T(8,128)(2,1)} %param.9), channel_id=1, source_target_pairs={{0,16},{8,24},{16,32},{24,40},{32,48},{40,56},{48,64},{56,72},{64,... | collective-permute-start | bytes 1474568 | tf_op jit(solution)/shard_map/ppermute | solution.py:14
  15.0 153.6 %collective-permute-start.2 = (bf16[384,640]{1,0:T(8,128)(2,1)}, bf16[384,640]{1,0:T(8,128)(2,1)S(1)}, u32[]{:S(2)}, u32[]{:S(2)}) collective-permute-start(bf16[384,640]{1,0:T(8,128)(2,1)} %param.9), channel_id=1, source_target_pairs={{0,24},{8,32},{16,40},{24,48},{32,56},{40,64},{48,72},{56,80},{64,... | collective-permute-start | bytes 1474568 | tf_op jit(solution)/shard_map/ppermute | solution.py:14
  18.4 152.5 %collective-permute-start.3 = (bf16[384,640]{1,0:T(8,128)(2,1)}, bf16[384,640]{1,0:T(8,128)(2,1)S(1)}, u32[]{:S(2)}, u32[]{:S(2)}) collective-permute-start(bf16[384,640]{1,0:T(8,128)(2,1)} %param.9), channel_id=1, source_target_pairs={{0,32},{8,40},{16,48},{24,56},{32,64},{40,72},{48,80},{56,88},{64,... | collective-permute-start | bytes 1474568 | tf_op jit(solution)/shard_map/ppermute | solution.py:14
  21.9 149.1 %collective-permute-start.4 = (bf16[384,640]{1,0:T(8,128)(2,1)}, bf16[384,640]{1,0:T(8,128)(2,1)S(1)}, u32[]{:S(2)}, u32[]{:S(2)}) collective-permute-start(bf16[384,640]{1,0:T(8,128)(2,1)} %param.10), channel_id=1, source_target_pairs={{0,8},{8,16},{16,24},{24,32},{32,40},{40,48},{48,56},{56,64},{64,7... | collective-permute-start | bytes 1474568 | tf_op jit(solution)/shard_map/ppermute | solution.py:14
  161.4 13.1 %collective-permute-start.5 = (bf16[384,640]{1,0:T(8,128)(2,1)}, bf16[384,640]{1,0:T(8,128)(2,1)S(1)}, u32[]{:S(2)}, u32[]{:S(2)}) collective-permute-start(bf16[384,640]{1,0:T(8,128)(2,1)} %param.10), channel_id=1, source_target_pairs={{0,16},{8,24},{16,32},{24,40},{32,48},{40,56},{48,64},{56,72},{64,... | collective-permute-start | bytes 1474568 | tf_op jit(solution)/shard_map/ppermute | solution.py:14
  163.8 21.1 %collective-permute-start.6 = (bf16[384,640]{1,0:T(8,128)(2,1)S(1)}, bf16[384,640]{1,0:T(8,128)(2,1)S(1)}, u32[]{:S(2)}, u32[]{:S(2)}) collective-permute-start(bf16[384,640]{1,0:T(8,128)(2,1)S(1)} %copy-done), channel_id=1, source_target_pairs={{0,24},{8,32},{16,40},{24,48},{32,56},{40,64},{48,72},{56,80},{64,... | collective-permute-start | bytes 1474568 | tf_op jit(solution)/shard_map/ppermute | solution.py:14
  168.6 26.9 %collective-permute-start.7 = (bf16[384,640]{1,0:T(8,128)(2,1)S(1)}, bf16[384,640]{1,0:T(8,128)(2,1)S(1)}, u32[]{:S(2)}, u32[]{:S(2)}) collective-permute-start(bf16[384,640]{1,0:T(8,128)(2,1)S(1)} %copy-done), channel_id=1, source_target_pairs={{0,32},{8,40},{16,48},{24,56},{32,64},{40,72},{48,80},{56,88},{64,... | collective-permute-start | bytes 1474568 | tf_op jit(solution)/shard_map/ppermute | solution.py:14
  170.9 24.8 %copy-start.1 = (bf16[384,640]{1,0:T(8,128)(2,1)S(1)}, bf16[384,640]{1,0:T(8,128)(2,1)}, u32[]{:S(2)}) copy-start(bf16[384,640]{1,0:T(8,128)(2,1)} %param.8) | copy-start | bytes 1474564
Sparse Core Ops, SparseCore 0:
  10.6 113.0 all-gather.1
  222.5 69.0 reduce-scatter.3
where the time goes:
time: 301 us; the launch traced here: 300 us
  blocking collectives  123 us (41%)
  waiting for transfers between devices  94.2 us (31%)
  starting transfers between devices  27.5 us (9%)
  matrix products  17.1 us (6%)
  between operations  17 us (6%)
  local copies, waits for them, and re-layouts  15.4 us (5%)
  other arithmetic  6.31 us (2%)
    all_gather x1, blocking collectives, on_device(): lax.all_gather(text_keys, 'tm', axis=0, tiled=True)  74.3 us
    unnamed x3, waiting for transfers between devices  70 us
    all_gather x1, blocking collectives, on_device(): lax.all_gather(text_values, 'tm', axis=0, tiled=True)  48.6 us
    ppermute x8, starting transfers between devices, from_behind(): lax.ppermute(value, axis, [(source, source + steps) for source in range(i...  27.5 us
    ppermute x8, waiting for transfers between devices, from_behind(): lax.ppermute(value, axis, [(source, source + steps) for source in range(i...  24.2 us
    unnamed x21, local copies, waits for them, and re-layouts  12.2 us
    dot_general x1, matrix products, on_device(): jnp.dot(attended_all, lax.all_gather(out_weight, 'tm', axis=1, tiled=True...  8.94 us
  transfers between devices with their start and end apart: 10, of which 4 were waited for; matrix products, arithmetic and copies ran while one was open for 7% of the time, Pallas kernels for 0%

commit v1 on v0

--- a/solution.py
+++ b/solution.py
@@ -21,7 +21,9 @@
     scale = 1.0 / math.sqrt(HD)
     position = lax.axis_index("tm")
     text_k, text_v = (
-        lax.all_gather(text_keys, "tm", axis=0, tiled=True),
+        jnp.concatenate(
+            lax.all_to_all(jnp.stack([text_keys] * lax.axis_size("tm")), "tm", 0, 0), axis=0
+        ),
         lax.all_gather(text_values, "tm", axis=0, tiled=True),
     )
     key_list = [keys]

time: 301 us -> 289 us (0.960)
  blocking collectives: 123 us -> 90.8 us
  local copies, waits for them, and re-layouts: 15.4 us -> 27.9 us
  starting transfers between devices: 27.5 us -> 36.8 us
  waiting for transfers between devices: 94.2 us -> 85.2 us
  matrix products: 17.1 us -> 23.5 us
    all_gather x1 -> x0, blocking collectives: 74.3 us -> none  [on_device(): lax.all_gather(text_keys, 'tm', axis=0, tiled=True)]
    all_gather x1, blocking collectives: 48.6 us -> 90.8 us  [on_device(): lax.all_gather(text_values, 'tm', axis=0, tiled=True)]
    unnamed x21, local copies, waits for them, and re-layouts: 12.2 us -> 21.1 us
    all_to_all x0 -> x1, starting transfers between devices: none -> 8.38 us  [on_device(): lax.all_to_all(jnp.stack([text_keys] * lax.axis_size('tm')), 'tm', 0, 0)]
    ppermute x8, waiting for transfers between devices: 24.2 us -> 16.2 us  [from_behind(): lax.ppermute(value, axis, [(source, source + steps) for source in range(i...]
    dot_general x5, matrix products: 3.71 us -> 9.22 us  [on_device(): jnp.dot(weights.astype(jnp.bfloat16), value_h, preferred_element_type=jnp...]
  transfers between devices with their start and end apart: 10 -> 11, of which waited for: 4 -> 3; matrix products, arithmetic and copies ran while one was open for 7% -> 14% of each run, Pallas kernels for 0% -> 0%
where the time goes in v1:
time: 289 us; the launch traced here: 287 us
  blocking collectives  90.8 us (31%)
  waiting for transfers between devices  85.2 us (29%)
  starting transfers between devices  36.8 us (13%)
  local copies, waits for them, and re-layouts  27.9 us (10%)
  matrix products  23.5 us (8%)
  between operations  16.8 us (6%)
  other arithmetic  6.31 us (2%)
    all_gather x1, blocking collectives, on_device(): lax.all_gather(text_values, 'tm', axis=0, tiled=True)  90.8 us
    unnamed x3, waiting for transfers between devices  69 us
    ppermute x8, starting transfers between devices, from_behind(): lax.ppermute(value, axis, [(source, source + steps) for source in range(i...  28.4 us
    unnamed x21, local copies, waits for them, and re-layouts  21.1 us
    ppermute x8, waiting for transfers between devices, from_behind(): lax.ppermute(value, axis, [(source, source + steps) for source in range(i...  16.2 us
    dot_general x5, matrix products, on_device(): jnp.dot(weights.astype(jnp.bfloat16), value_h, preferred_element_type=jnp...  9.22 us
    dot_general x1, matrix products, on_device(): jnp.dot(attended_all, lax.all_gather(out_weight, 'tm', axis=1, tiled=True...  8.93 us
    all_to_all x1, starting transfers between devices, on_device(): lax.all_to_all(jnp.stack([text_keys] * lax.axis_size('tm')), 'tm', 0, 0)  8.38 us
  transfers between devices with their start and end apart: 11, of which 3 were waited for; matrix products, arithmetic and copies ran while one was open for 14% of the time, Pallas kernels for 0%

profile of v1, /device:TPU:1, one launch (start us, length us, event | category | flops | bytes accessed | tf_op | source)
XLA Modules:
  0.0 287.2 jit_solution(8477077985667173023)
XLA Ops:
  7.3 4.5 %collective-permute-start = (bf16[384,640]{1,0:T(8,128)(2,1)}, bf16[384,640]{1,0:T(8,128)(2,1)}, u32[]{:S(2)}, u32[]{:S(2)}) collective-permute-start(bf16[384,640]{1,0:T(8,128)(2,1)} %param.9), channel_id=1, source_target_pairs={{0,8},{8,16},{16,24},{24,32},{32,40},{40,48},{48,56},{56,64},{64,7... | collective-permute-start | bytes 1474568 | tf_op jit(solution)/shard_map/ppermute | solution.py:14
  11.8 3.9 %collective-permute-start.1 = (bf16[384,640]{1,0:T(8,128)(2,1)}, bf16[384,640]{1,0:T(8,128)(2,1)}, u32[]{:S(2)}, u32[]{:S(2)}) collective-permute-start(bf16[384,640]{1,0:T(8,128)(2,1)} %param.9), channel_id=1, source_target_pairs={{0,16},{8,24},{16,32},{24,40},{32,48},{40,56},{48,64},{56,72},{64,... | collective-permute-start | bytes 1474568 | tf_op jit(solution)/shard_map/ppermute | solution.py:14
  15.7 3.5 %collective-permute-start.2 = (bf16[384,640]{1,0:T(8,128)(2,1)}, bf16[384,640]{1,0:T(8,128)(2,1)}, u32[]{:S(2)}, u32[]{:S(2)}) collective-permute-start(bf16[384,640]{1,0:T(8,128)(2,1)} %param.9), channel_id=1, source_target_pairs={{0,24},{8,32},{16,40},{24,48},{32,56},{40,64},{48,72},{56,80},{64,... | collective-permute-start | bytes 1474568 | tf_op jit(solution)/shard_map/ppermute | solution.py:14
  19.2 3.5 %collective-permute-start.3 = (bf16[384,640]{1,0:T(8,128)(2,1)}, bf16[384,640]{1,0:T(8,128)(2,1)}, u32[]{:S(2)}, u32[]{:S(2)}) collective-permute-start(bf16[384,640]{1,0:T(8,128)(2,1)} %param.9), channel_id=1, source_target_pairs={{0,32},{8,40},{16,48},{24,56},{32,64},{40,72},{48,80},{56,88},{64,... | collective-permute-start | bytes 1474568 | tf_op jit(solution)/shard_map/ppermute | solution.py:14
  22.6 1.6 stack.2
  24.3 8.4 %all-to-all-start = ((bf16[64,8,640]{2,1,0:T(8,128)(2,1)}), bf16[64,8,640]{2,1,0:T(8,128)(2,1)}, u32[]{:S(2)}, u32[]{:S(2)}) async-start(bf16[64,8,640]{2,1,0:T(8,128)(2,1)} %stack.2), calls=%async_computation | async-start | bytes 1310720 | tf_op jit(solution)/shard_map/all_to_all | solution.py:25
  32.7 3.5 %collective-permute-start.4 = (bf16[384,640]{1,0:T(8,128)(2,1)}, bf16[384,640]{1,0:T(8,128)(2,1)}, u32[]{:S(2)}, u32[]{:S(2)}) collective-permute-start(bf16[384,640]{1,0:T(8,128)(2,1)} %param.10), channel_id=1, source_target_pairs={{0,8},{8,16},{16,24},{24,32},{32,40},{40,48},{48,56},{56,64},{64,7... | collective-permute-start | bytes 1474568 | tf_op jit(solution)/shard_map/ppermute | solution.py:14
  42.1 90.8 %all_gather.6 = bf16[512,640]{1,0:T(8,128)(2,1)} all-gather(bf16[8,640]{1,0:T(8,128)(2,1)} %param.12), channel_id=1, replica_groups=mesh['tm'=64,'head'=8] {'tm'}, dimensions={0}, use_global_device_ids=true | all-gather | bytes 665600 | tf_op jit(solution)/shard_map/all_gather | solution.py:27
  138.6 1.9 constant_dynamic-update-slice_fusion.10
  143.0 4.8 %collective-permute-start.6 = (bf16[384,640]{1,0:T(8,128)(2,1)}, bf16[384,640]{1,0:T(8,128)(2,1)S(1)}, u32[]{:S(2)}, u32[]{:S(2)}) collective-permute-start(bf16[384,640]{1,0:T(8,128)(2,1)} %param.10), channel_id=1, source_target_pairs={{0,24},{8,32},{16,40},{24,48},{32,56},{40,64},{48,72},{56,80},{64,... | collective-permute-start | bytes 1474568 | tf_op jit(solution)/shard_map/ppermute | solution.py:14
  148.9 3.2 %collective-permute-start.7 = (bf16[384,640]{1,0:T(8,128)(2,1)}, bf16[384,640]{1,0:T(8,128)(2,1)S(1)}, u32[]{:S(2)}, u32[]{:S(2)}) collective-permute-start(bf16[384,640]{1,0:T(8,128)(2,1)} %param.10), channel_id=1, source_target_pairs={{0,32},{8,40},{16,48},{24,56},{32,64},{40,72},{48,80},{56,88},{64,... | collective-permute-start | bytes 1474568 | tf_op jit(solution)/shard_map/ppermute | solution.py:14
  154.3 1.9 constant_dynamic-update-slice_fusion.9
  157.0 6.5 %collective-permute-done.6 = bf16[384,640]{1,0:T(8,128)(2,1)S(1)} collective-permute-done((bf16[384,640]{1,0:T(8,128)(2,1)}, bf16[384,640]{1,0:T(8,128)(2,1)S(1)}, u32[]{:S(2)}, u32[]{:S(2)}) %collective-permute-start.6) | collective-permute-done | bytes 491552 | tf_op jit(solution)/shard_map/ppermute | solution.py:14
  164.4 9.7 %collective-permute-done.7 = bf16[384,640]{1,0:T(8,128)(2,1)S(1)} collective-permute-done((bf16[384,640]{1,0:T(8,128)(2,1)}, bf16[384,640]{1,0:T(8,128)(2,1)S(1)}, u32[]{:S(2)}, u32[]{:S(2)}) %collective-permute-start.7) | collective-permute-done | bytes 491552 | tf_op jit(solution)/shard_map/ppermute | solution.py:14
  177.1 1.8 fusion.96
  185.5 1.9 fusion.72
  187.4 1.8 fusion.66
  189.2 1.8 fusion.60
  191.1 1.8 fusion.54
  192.9 1.8 fusion.48
  194.8 8.9 %convolution_convert_fusion = bf16[384,5120]{1,0:T(8,128)(2,1)} fusion(bf16[384,640]{1,0:T(8,128)(2,1)S(1)} %fusion.48, bf16[640,5120]{0,1:T(8,128)(2,1)} %all-gather.2.cloned.1.call-done), kind=kOutput, calls=%fused_computation | convolution fusion | flops 2518548480 | bytes 10977280 | tf_op jit(solution)/shard_map/dot_general | solution.py:69
  203.8 6.3 %copy.9 = bf16[384,5120]{0,1:T(8,128)(2,1)} copy(bf16[384,5120]{1,0:T(8,128)(2,1)} %convolution_convert_fusion) | data formatting | bytes 7864320
  210.0 68.3 %reduce-scatter.4.cloned.1.call-done = bf16[640,384]{1,0:T(8,128)(2,1)} async-done(((bf16[5120,384]{1,0:T(8,128)(2,1)}), bf16[640,384]{1,0:T(8,128)(2,1)}) %reduce-scatter.4.cloned.1.call-update) | async-done | bytes 491536
  278.4 2.0 copy.10
  (51 shorter events, 26.3 us)
Async XLA Ops:
  6.5 188.3 %all-gather.2.cloned.1.call-start = ((), (), s32[]{:S(2)}) async-start(), calls=%async_computation.2 | async-start | bytes 6656000 | tf_op jit(solution)/shard_map/all_gather | solution.py:71
  7.3 133.2 %collective-permute-start = (bf16[384,640]{1,0:T(8,128)(2,1)}, bf16[384,640]{1,0:T(8,128)(2,1)}, u32[]{:S(2)}, u32[]{:S(2)}) collective-permute-start(bf16[384,640]{1,0:T(8,128)(2,1)} %param.9), channel_id=1, source_target_pairs={{0,8},{8,16},{16,24},{24,32},{32,40},{40,48},{48,56},{56,64},{64,7... | collective-permute-start | bytes 1474568 | tf_op jit(solution)/shard_map/ppermute | solution.py:14
  11.8 131.2 %collective-permute-start.1 = (bf16[384,640]{1,0:T(8,128)(2,1)}, bf16[384,640]{1,0:T(8,128)(2,1)}, u32[]{:S(2)}, u32[]{:S(2)}) collective-permute-start(bf16[384,640]{1,0:T(8,128)(2,1)} %param.9), channel_id=1, source_target_pairs={{0,16},{8,24},{16,32},{24,40},{32,48},{40,56},{48,64},{56,72},{64,... | collective-permute-start | bytes 1474568 | tf_op jit(solution)/shard_map/ppermute | solution.py:14
  15.7 133.2 %collective-permute-start.2 = (bf16[384,640]{1,0:T(8,128)(2,1)}, bf16[384,640]{1,0:T(8,128)(2,1)}, u32[]{:S(2)}, u32[]{:S(2)}) collective-permute-start(bf16[384,640]{1,0:T(8,128)(2,1)} %param.9), channel_id=1, source_target_pairs={{0,24},{8,32},{16,40},{24,48},{32,56},{40,64},{48,72},{56,80},{64,... | collective-permute-start | bytes 1474568 | tf_op jit(solution)/shard_map/ppermute | solution.py:14
  19.2 134.1 %collective-permute-start.3 = (bf16[384,640]{1,0:T(8,128)(2,1)}, bf16[384,640]{1,0:T(8,128)(2,1)}, u32[]{:S(2)}, u32[]{:S(2)}) collective-permute-start(bf16[384,640]{1,0:T(8,128)(2,1)} %param.9), channel_id=1, source_target_pairs={{0,32},{8,40},{16,48},{24,56},{32,64},{40,72},{48,80},{56,88},{64,... | collective-permute-start | bytes 1474568 | tf_op jit(solution)/shard_map/ppermute | solution.py:14
  24.3 151.6 %all-to-all-start = ((bf16[64,8,640]{2,1,0:T(8,128)(2,1)}), bf16[64,8,640]{2,1,0:T(8,128)(2,1)}, u32[]{:S(2)}, u32[]{:S(2)}) async-start(bf16[64,8,640]{2,1,0:T(8,128)(2,1)} %stack.2), calls=%async_computation | async-start | bytes 1310720 | tf_op jit(solution)/shard_map/all_to_all | solution.py:25
  32.6 245.7 %reduce-scatter.4.cloned.1.call-start = ((), (), s32[]{:S(2)}) async-start(), calls=%async_computation.3 | async-start | bytes 4423680
  32.7 121.6 %collective-permute-start.4 = (bf16[384,640]{1,0:T(8,128)(2,1)}, bf16[384,640]{1,0:T(8,128)(2,1)}, u32[]{:S(2)}, u32[]{:S(2)}) collective-permute-start(bf16[384,640]{1,0:T(8,128)(2,1)} %param.10), channel_id=1, source_target_pairs={{0,8},{8,16},{16,24},{24,32},{32,40},{40,48},{48,56},{56,64},{64,7... | collective-permute-start | bytes 1474568 | tf_op jit(solution)/shard_map/ppermute | solution.py:14
  140.5 34.4 %copy-start = (bf16[512,640]{1,0:T(8,128)(2,1)S(1)}, bf16[512,640]{1,0:T(8,128)(2,1)}, u32[]{:S(2)}) copy-start(bf16[512,640]{1,0:T(8,128)(2,1)} %all_gather.6) | copy-start | bytes 1966084
  140.5 15.7 %collective-permute-start.5 = (bf16[384,640]{1,0:T(8,128)(2,1)}, bf16[384,640]{1,0:T(8,128)(2,1)S(1)}, u32[]{:S(2)}, u32[]{:S(2)}) collective-permute-start(bf16[384,640]{1,0:T(8,128)(2,1)} %param.10), channel_id=1, source_target_pairs={{0,16},{8,24},{16,32},{24,40},{32,48},{40,56},{48,64},{56,72},{64,... | collective-permute-start | bytes 1474568 | tf_op jit(solution)/shard_map/ppermute | solution.py:14
  143.0 20.5 %collective-permute-start.6 = (bf16[384,640]{1,0:T(8,128)(2,1)}, bf16[384,640]{1,0:T(8,128)(2,1)S(1)}, u32[]{:S(2)}, u32[]{:S(2)}) collective-permute-start(bf16[384,640]{1,0:T(8,128)(2,1)} %param.10), channel_id=1, source_target_pairs={{0,24},{8,32},{16,40},{24,48},{32,56},{40,64},{48,72},{56,80},{64,... | collective-permute-start | bytes 1474568 | tf_op jit(solution)/shard_map/ppermute | solution.py:14
  148.9 25.1 %collective-permute-start.7 = (bf16[384,640]{1,0:T(8,128)(2,1)}, bf16[384,640]{1,0:T(8,128)(2,1)S(1)}, u32[]{:S(2)}, u32[]{:S(2)}) collective-permute-start(bf16[384,640]{1,0:T(8,128)(2,1)} %param.10), channel_id=1, source_target_pairs={{0,32},{8,40},{16,48},{24,56},{32,64},{40,72},{48,80},{56,88},{64,... | collective-permute-start | bytes 1474568 | tf_op jit(solution)/shard_map/ppermute | solution.py:14
  177.0 2.5 copy-start.1
Sparse Core Ops, SparseCore 0:
  10.6 115.6 all-gather.1
  210.2 68.1 reduce-scatter.3
